TPU v7x, 512 devices: a whole 4x4x16 slice. The times are simulated.
512 devices in a mesh: seq: 64 (over x, z), head: 8 (over y, core).
Axes of the slice: x: 4, y: 4, z: 16, core: 2. Of those that a mesh axis runs over, the one named last changes fastest.
Arguments:
- tokens: bfloat16 [16384, 4096], P('seq', 'head'), may hold values from -40 to 40
- queries: bfloat16 [16384, 4096], P('seq', 'head'), may hold values from -6 to 6
- key_rows: bfloat16 [16384, 4096], P('seq', 'head'), may hold values from -6 to 6
- values: bfloat16 [16384, 4096], P('seq', 'head'), may hold values from -6 to 6
- log_decay: float32 [32, 16384], P('head', 'seq'), may hold values from -1 to 0
- head_gain: float32 [4096], P('head'), may hold values from 0.5 to 1.5
- expert_gain: float32 [4096], P('head'), may hold values from 0.5 to 1.5
- route_ids: int32 [16384, 2], P('seq'), may hold values from 0 to 31, all different within a row; in each aligned block of 256 rows (0 to 255, 256 to 511, ...) at most 20 rows name the same one
- route_weight: float32 [16384, 2], P('seq'), may hold values from 0.2 to 1
- expert_in: bfloat16 [64, 4096, 1408], P('seq', 'head'), may hold values from -0.09375 to 0.09375
- expert_out: bfloat16 [64, 704, 4096], P('seq', None, 'head'), may hold values from -0.15625 to 0.15625
Outputs:
- mixed: bfloat16 [16384, 4096], P('seq', 'head')
Inputs may be any that keep to these rules, and one draw needn't show every extreme that they name: `route_ids`: within the rows of one device (aligned blocks of 256 tokens) no expert is named by more than 20 tokens, a bound that some block reaches; a token's two experts differ.
All inputs are finite; a program needn't handle non-finite values.
Results may differ from a plain program's by a relative error of at most 0.015.
Values may be sent and summed in bfloat16 or wider, within the bound.
No kernel may reach another device: no remote copies, remote signals or barrier semaphores. Data moves between devices by JAX's collectives and lax.ppermute only.
A program may use at most 64 MiB of HBM per device.

v0:
```python
import jax
import jax.numpy as jnp
from jax import lax
from jax.sharding import PartitionSpec as P

D = 4096
EXPERTS = 32
CAP = 20
EPSILON = 1e-06


def pack_window(decay, state):
    heads, rows, cols = state.shape
    high = decay.astype(jnp.bfloat16)
    low = (decay - high.astype(jnp.float32)).astype(jnp.bfloat16)
    tail = jnp.broadcast_to(jnp.stack([high, low], axis=1)[:, :, None], (heads, 2, cols))
    return jnp.concatenate([state.astype(jnp.bfloat16), tail], axis=1)


def exclusive_scan(decay, state, axis):
    place = lax.axis_index(axis)
    count = lax.axis_size(axis)
    rows = state.shape[1]
    window_decay = decay
    window_state = state
    before_decay = jnp.ones_like(decay)
    before_state = jnp.zeros_like(state)
    shift = 1
    while shift < count:
        pairs = [(j, j + shift) for j in range(count - shift)]
        got = lax.ppermute(pack_window(window_decay, window_state), axis, pairs)
        valid = place >= shift
        got_state = got[:, :rows, :].astype(jnp.float32)
        got_decay = got[:, rows, 0].astype(jnp.float32) + got[:, rows + 1, 0].astype(jnp.float32)
        got_decay = jnp.where(valid, got_decay, 1.0)
        before_state = before_decay[:, None, None] * got_state + before_state
        before_decay = before_decay * got_decay
        window_state = window_decay[:, None, None] * got_state + window_state
        window_decay = window_decay * got_decay
        shift *= 2
    return before_state


def head_reduce_activate(partial, axis, block_units):
    place = lax.axis_index(axis)
    count = lax.axis_size(axis)
    chips = count // 2
    core = place % 2
    chip = place // 2
    blocks_here, rows, width = partial.shape
    share = rows // count
    pieces = partial.reshape(blocks_here, chips, 2, share, width)
    sibling = [(j, j ^ 1) for j in range(count)]
    kept = lax.dynamic_index_in_dim(pieces, core, 2, False).astype(jnp.float32)
    handed = lax.dynamic_index_in_dim(pieces, 1 - core, 2, False)
    pair_sum = kept + lax.ppermute(handed, axis, sibling).astype(jnp.float32)
    total = lax.dynamic_index_in_dim(pair_sum, chip, 1, False)
    for step in range(1, chips):
        target = (chip + step) % chips
        outgoing = lax.dynamic_index_in_dim(pair_sum, target, 1, False).astype(jnp.bfloat16)
        pairs = [(j, (j + 2 * step) % count) for j in range(count)]
        total = total + lax.ppermute(outgoing, axis, pairs).astype(jnp.float32)
    split = total.reshape(blocks_here, share, width // (2 * block_units), 2, block_units)
    mine = (jax.nn.silu(split[:, :, :, 0]) * split[:, :, :, 1]).astype(jnp.bfloat16)
    mine = mine.reshape(blocks_here, share, width // 2)
    gathered = [mine]
    for step in range(1, chips):
        pairs = [(j, (j + 2 * step) % count) for j in range(count)]
        gathered.append(lax.ppermute(mine, axis, pairs))
    stacked = jnp.stack(gathered, axis=1)
    reverse = stacked[:, ::-1]
    doubled = jnp.concatenate([reverse, reverse], axis=1)
    ordered = lax.dynamic_slice_in_dim(doubled, (chips - 1 - chip) % chips, chips, 1)
    other = lax.ppermute(ordered, axis, sibling)
    three = jnp.stack([ordered, other, ordered], axis=2)
    full = lax.dynamic_slice_in_dim(three, core, 2, 2)
    return full.reshape(blocks_here, rows, width // 2)


def per_device(
    tokens,
    queries,
    key_rows,
    values,
    log_decay,
    head_gain,
    expert_gain,
    route_ids,
    route_weight,
    expert_in,
    expert_out,
):
    parity = lax.axis_index("seq") % 2
    partner = [(j, j ^ 1) for j in range(lax.axis_size("seq"))]
    other_in = lax.ppermute(expert_in, "seq", partner)
    other_out = lax.ppermute(expert_out, "seq", partner)
    length = tokens.shape[0]
    local_width = tokens.shape[1]
    heads_here = log_decay.shape[0]
    head_size = queries.shape[1] // heads_here
    score_scale = head_size ** (-0.5)
    query_heads = queries.reshape(length, heads_here, head_size)
    key_heads = key_rows.reshape(length, heads_here, head_size)
    value_heads = values.reshape(length, heads_here, head_size)
    cumulative = jnp.cumsum(log_decay, axis=1)
    causal = (jnp.arange(length)[:, None] >= jnp.arange(length)[None, :])[None]
    scores = (
        jnp.einsum("thd,shd->hts", query_heads, key_heads, preferred_element_type=jnp.float32)
        * score_scale
    )
    spread = cumulative[:, :, None] - cumulative[:, None, :]
    mixing = jnp.where(causal, scores * jnp.exp(jnp.where(causal, spread, 0.0)), 0.0).astype(
        jnp.bfloat16
    )
    inside = jnp.einsum("hts,shd->thd", mixing, value_heads, preferred_element_type=jnp.float32)
    to_end = jnp.exp(cumulative[:, -1:] - cumulative)
    carried_keys = (key_heads.astype(jnp.float32) * to_end.T[:, :, None]).astype(jnp.bfloat16)
    block_state = jnp.einsum(
        "shd,she->hde", carried_keys, value_heads, preferred_element_type=jnp.float32
    )
    block_decay = jnp.exp(cumulative[:, -1])
    entering = exclusive_scan(block_decay, block_state, "seq")
    entering, other_in = lax.optimization_barrier((entering, other_in))
    from_before = jnp.einsum(
        "thd,hde->the",
        query_heads.astype(jnp.float32),
        entering,
        precision=lax.Precision.HIGHEST,
        preferred_element_type=jnp.float32,
    )
    attended = inside + from_before * (jnp.exp(cumulative).T[:, :, None] * score_scale)
    head_rms = lax.rsqrt(jnp.mean(attended * attended, axis=2, keepdims=True) + EPSILON)
    normed_heads = (attended * head_rms).reshape(length, local_width)
    hidden_state = (tokens.astype(jnp.float32) + normed_heads * head_gain).astype(jnp.bfloat16)
    hidden_wide = hidden_state.astype(jnp.float32)
    local_squares = jnp.sum(hidden_wide * hidden_wide, axis=1)
    total_squares = lax.psum(local_squares, "head")
    inverse_rms = lax.rsqrt(total_squares / D + EPSILON)
    expert_input = (hidden_wide * inverse_rms[:, None] * expert_gain).astype(jnp.bfloat16)
    capacity = CAP
    expert_count = EXPERTS
    flat_ids = route_ids.reshape(-1)
    pair_count = flat_ids.shape[0]
    chosen = (flat_ids[:, None] == jnp.arange(expert_count)[None, :]).astype(jnp.float32)
    strictly_before = (jnp.arange(pair_count)[:, None] > jnp.arange(pair_count)[None, :]).astype(
        jnp.float32
    )
    earlier_counts = jnp.dot(
        strictly_before, chosen, precision=lax.Precision.HIGHEST, preferred_element_type=jnp.float32
    )
    slot_index = jnp.sum(earlier_counts * chosen, axis=1).astype(jnp.int32)
    position = (flat_ids * capacity + slot_index).reshape(length, route_ids.shape[1])
    slot_ids = jnp.arange(expert_count * capacity, dtype=jnp.int32)
    picks = position[None, :, :] == slot_ids[:, None, None]
    dispatch_matrix = jnp.any(picks, axis=2).astype(jnp.bfloat16)
    send_rows = jnp.dot(dispatch_matrix, expert_input, preferred_element_type=jnp.float32).astype(
        jnp.bfloat16
    )
    half = capacity // 2
    block_units = expert_out.shape[1]
    send_buffer = send_rows.reshape(expert_count * 2, 1, half, local_width)
    arrived = lax.all_to_all(send_buffer, "seq", split_axis=0, concat_axis=1, tiled=True)
    blocks_here, sources = (arrived.shape[0], arrived.shape[1])
    flat_rows = arrived.reshape(blocks_here, sources * half, local_width)
    own_sums = jnp.einsum(
        "erd,edh->erh", flat_rows, expert_in, preferred_element_type=jnp.float32
    ).astype(jnp.bfloat16)
    other_sums = jnp.einsum(
        "erd,edh->erh", flat_rows, other_in, preferred_element_type=jnp.float32
    ).astype(jnp.bfloat16)
    partial_sums = jnp.concatenate([own_sums, other_sums], axis=2)
    activated = head_reduce_activate(partial_sums, "head", block_units)
    activated, other_out = lax.optimization_barrier((activated, other_out))
    activated = activated.reshape(blocks_here, sources * half, 2, block_units)
    weight_out = jnp.stack([expert_out, other_out], axis=1)
    summed = jnp.einsum(
        "erkh,ekhd->erd", activated, weight_out, preferred_element_type=jnp.float32
    ).astype(jnp.bfloat16)
    summed = summed.reshape(blocks_here, sources, half, local_width)
    returned = lax.all_to_all(summed, "seq", split_axis=1, concat_axis=0, tiled=True)
    merged = returned.reshape(expert_count, capacity, local_width).astype(jnp.float32)
    merged = merged.reshape(expert_count * capacity, local_width)
    slot_rows = merged[position]
    expert_mix = jnp.sum(slot_rows * route_weight[:, :, None], axis=1)
    return (hidden_wide + expert_mix).astype(jnp.bfloat16)


def solution(mesh):
    return jax.shard_map(
        per_device,
        mesh=mesh,
        in_specs=(
            P("seq", "head"),
            P("seq", "head"),
            P("seq", "head"),
            P("seq", "head"),
            P("head", "seq"),
            P("head"),
            P("head"),
            P("seq", None),
            P("seq", None),
            P("seq", "head", None),
            P("seq", None, "head"),
        ),
        out_specs=P("seq", "head"),
        check_vma=False,
    )
```

profile of v0, /device:TPU:6, one launch (start us, length us, event | category | flops | bytes accessed | tf_op | source)
XLA Modules:
  0.0 340.9 jit_solution(1136357605575012222)
XLA Ops:
  1.8 1.2 reduce-window.6
  5.1 3.8 %collective-permute-start = (bf16[4,130,128]{2,1,0:T(8,128)(2,1)S(1)}, bf16[4,130,128]{2,1,0:T(8,128)(2,1)S(1)}, u32[]{:S(2)}, u32[]{:S(2)}) collective-permute-start(bf16[4,130,128]{2,1,0:T(8,128)(2,1)S(1)} %pad_maximum_fusion.1), channel_id=1, source_target_pairs={{0,8},{8,16},{16,24},{24,32},{32,40},{40,48},{48,56},{56,64},{64,7... | collective-permute-start | bytes 399368 | tf_op jit(solution)/shard_map/ppermute | solution.py:31
  9.0 11.5 %collective-permute-done = bf16[4,130,128]{2,1,0:T(8,128)(2,1)S(1)} collective-permute-done((bf16[4,130,128]{2,1,0:T(8,128)(2,1)S(1)}, bf16[4,130,128]{2,1,0:T(8,128)(2,1)S(1)}, u32[]{:S(2)}, u32[]{:S(2)}) %collective-permute-start) | collective-permute-done | bytes 133152 | tf_op jit(solution)/shard_map/ppermute | solution.py:31
  20.9 1.9 collective-permute-start.1
  22.9 10.1 %collective-permute-done.1 = bf16[4,130,128]{2,1,0:T(8,128)(2,1)S(1)} collective-permute-done((bf16[4,130,128]{2,1,0:T(8,128)(2,1)S(1)}, bf16[4,130,128]{2,1,0:T(8,128)(2,1)S(1)}, u32[]{:S(2)}, u32[]{:S(2)}) %collective-permute-start.1) | collective-permute-done | bytes 133152 | tf_op jit(solution)/shard_map/ppermute | solution.py:31
  33.7 1.9 collective-permute-start.2
  35.6 15.3 %collective-permute-done.2 = bf16[4,130,128]{2,1,0:T(8,128)(2,1)S(1)} collective-permute-done((bf16[4,130,128]{2,1,0:T(8,128)(2,1)S(1)}, bf16[4,130,128]{2,1,0:T(8,128)(2,1)S(1)}, u32[]{:S(2)}, u32[]{:S(2)}) %collective-permute-start.2) | collective-permute-done | bytes 133152 | tf_op jit(solution)/shard_map/ppermute | solution.py:31
  51.5 1.9 collective-permute-start.3
  53.4 6.7 %collective-permute-start.6 = (bf16[1,512,1408]{2,1,0:T(8,128)(2,1)}, bf16[1,512,1408]{2,1,0:T(8,128)(2,1)}, u32[]{:S(2)}, u32[]{:S(2)}) collective-permute-start(bf16[1,512,1408]{2,1,0:T(8,128)(2,1)} %param.20), channel_id=1, source_target_pairs={{0,8},{8,0},{16,24},{24,16},{32,40},{40,32},{48,56},{56,48},{64,72... | collective-permute-start | bytes 4325384 | tf_op jit(solution)/shard_map/ppermute | solution.py:95
  60.2 11.1 %collective-permute-done.3 = bf16[4,130,128]{2,1,0:T(8,128)(2,1)S(1)} collective-permute-done((bf16[4,130,128]{2,1,0:T(8,128)(2,1)S(1)}, bf16[4,130,128]{2,1,0:T(8,128)(2,1)S(1)}, u32[]{:S(2)}, u32[]{:S(2)}) %collective-permute-start.3) | collective-permute-done | bytes 133152 | tf_op jit(solution)/shard_map/ppermute | solution.py:31
  71.8 1.3 collective-permute-start.4
  74.5 4.5 %collective-permute-done.4 = bf16[4,130,128]{2,1,0:T(8,128)(2,1)S(1)} collective-permute-done((bf16[4,130,128]{2,1,0:T(8,128)(2,1)S(1)}, bf16[4,130,128]{2,1,0:T(8,128)(2,1)S(1)}, u32[]{:S(2)}, u32[]{:S(2)}) %collective-permute-start.4) | collective-permute-done | bytes 133152 | tf_op jit(solution)/shard_map/ppermute | solution.py:31
  79.5 1.3 collective-permute-start.5
  81.0 6.9 %collective-permute-done.5 = bf16[4,130,128]{2,1,0:T(8,128)(2,1)S(1)} collective-permute-done((bf16[4,130,128]{2,1,0:T(8,128)(2,1)S(1)}, bf16[4,130,128]{2,1,0:T(8,128)(2,1)S(1)}, u32[]{:S(2)}, u32[]{:S(2)}) %collective-permute-start.5) | collective-permute-done | bytes 133152 | tf_op jit(solution)/shard_map/ppermute | solution.py:31
  88.2 8.4 %collective-permute-done.6 = bf16[1,512,1408]{2,1,0:T(8,128)(2,1)} collective-permute-done((bf16[1,512,1408]{2,1,0:T(8,128)(2,1)}, bf16[1,512,1408]{2,1,0:T(8,128)(2,1)}, u32[]{:S(2)}, u32[]{:S(2)}) %collective-permute-start.6) | collective-permute-done | bytes 1441824 | tf_op jit(solution)/shard_map/ppermute | solution.py:95
  97.7 12.4 %psum.7 = f32[256]{0:T(256)S(1)} all-reduce(f32[256]{0:T(256)S(1)} %get-tuple-element.25), channel_id=1, replica_groups=mesh['seq'=64,'head'=8] {'head'}, use_global_device_ids=true, to_apply=%region_6.7 | all-reduce | flops 256 | bytes 2048 | tf_op jit(solution)/shard_map/psum | solution.py:137
  111.7 13.4 %all-to-all-start = ((bf16[64,1,10,512]{3,2,1,0:T(8,128)(2,1)}), bf16[64,1,10,512]{3,2,1,0:T(8,128)(2,1)S(1)}, u32[]{:S(2)}, u32[]{:S(2)}) async-start(bf16[64,1,10,512]{3,2,1,0:T(8,128)(2,1)} %bitcast.8), calls=%async_computation | async-start | bytes 2097152 | tf_op jit(solution)/shard_map/all_to_all | solution.py:162
  125.1 50.7 %all-to-all-done = bf16[64,1,10,512]{3,2,1,0:T(8,128)(2,1)S(1)} async-done(((bf16[64,1,10,512]{3,2,1,0:T(8,128)(2,1)}), bf16[64,1,10,512]{3,2,1,0:T(8,128)(2,1)S(1)}, u32[]{:S(2)}, u32[]{:S(2)}) %all-to-all-start) | async-done | bytes 655392 | tf_op jit(solution)/shard_map/all_to_all | solution.py:162
  176.1 2.5 convolution_convert_fusion.1
  178.6 2.5 convolution_convert_fusion
  181.2 1.5 fusion.3
  183.0 1.9 collective-permute-start.7
  185.0 4.0 %collective-permute-done.7 = bf16[1,4,80,2816]{3,2,1,0:T(8,128)(2,1)} collective-permute-done((bf16[1,4,80,2816]{3,2,1,0:T(8,128)(2,1)}, bf16[1,4,80,2816]{3,2,1,0:T(8,128)(2,1)}, u32[]{:S(2)}, u32[]{:S(2)}) %collective-permute-start.7) | collective-permute-done | bytes 1802272 | tf_op jit(solution)/shard_map/ppermute | solution.py:56
  188.9 2.1 convert_add_fusion
  191.0 1.8 copy-done.1
  192.9 1.9 collective-permute-start.10
  194.8 3.7 %collective-permute-start.9 = (bf16[1,80,2816]{2,1,0:T(8,128)(2,1)S(1)}, bf16[1,80,2816]{2,1,0:T(8,128)(2,1)S(1)}, u32[]{:S(2)}, u32[]{:S(2)}) collective-permute-start(bf16[1,80,2816]{2,1,0:T(8,128)(2,1)S(1)} %get-tuple-element.45), channel_id=1, source_target_pairs={{0,4},{1,5},{2,6},{3,7},{4,0},{5,1},{6,2},{7,3},{8,12},{9,13},{10,... | collective-permute-start | bytes 1351688 | tf_op jit(solution)/shard_map/ppermute | solution.py:62
  198.5 3.4 collective-permute-start.8
  202.0 6.0 %collective-permute-done.10 = bf16[1,80,2816]{2,1,0:T(8,128)(2,1)S(1)} collective-permute-done((bf16[1,80,2816]{2,1,0:T(8,128)(2,1)S(1)}, bf16[1,80,2816]{2,1,0:T(8,128)(2,1)S(1)}, u32[]{:S(2)}, u32[]{:S(2)}) %collective-permute-start.10) | collective-permute-done | bytes 450592 | tf_op jit(solution)/shard_map/ppermute | solution.py:62
  208.0 3.5 %collective-permute-done.9 = bf16[1,80,2816]{2,1,0:T(8,128)(2,1)S(1)} collective-permute-done((bf16[1,80,2816]{2,1,0:T(8,128)(2,1)S(1)}, bf16[1,80,2816]{2,1,0:T(8,128)(2,1)S(1)}, u32[]{:S(2)}, u32[]{:S(2)}) %collective-permute-start.9) | collective-permute-done | bytes 450592 | tf_op jit(solution)/shard_map/ppermute | solution.py:62
  211.5 8.8 %collective-permute-done.8 = bf16[1,80,2816]{2,1,0:T(8,128)(2,1)S(1)} collective-permute-done((bf16[1,80,2816]{2,1,0:T(8,128)(2,1)S(1)}, bf16[1,80,2816]{2,1,0:T(8,128)(2,1)S(1)}, u32[]{:S(2)}, u32[]{:S(2)}) %collective-permute-start.8) | collective-permute-done | bytes 450592 | tf_op jit(solution)/shard_map/ppermute | solution.py:62
  220.3 1.4 fusion.27
  224.8 2.5 collective-permute-start.13
  227.3 3.6 %collective-permute-start.12 = (bf16[1,80,1408]{2,1,0:T(8,128)(2,1)S(1)}, bf16[1,80,1408]{2,1,0:T(8,128)(2,1)S(1)}, u32[]{:S(2)}, u32[]{:S(2)}) collective-permute-start(bf16[1,80,1408]{2,1,0:T(8,128)(2,1)S(1)} %multiply_convert_fusion.1), channel_id=1, source_target_pairs={{0,4},{1,5},{2,6},{3,7},{4,0},{5,1},{6,2},{7,3},{8,12},{9,13},{10,... | collective-permute-start | bytes 675848 | tf_op jit(solution)/shard_map/ppermute | solution.py:69
  230.9 2.7 collective-permute-start.11
  235.1 3.3 collective-permute-done.12
  238.3 4.0 %collective-permute-done.11 = bf16[1,80,1408]{2,1,0:T(8,128)(2,1)S(1)} collective-permute-done((bf16[1,80,1408]{2,1,0:T(8,128)(2,1)S(1)}, bf16[1,80,1408]{2,1,0:T(8,128)(2,1)S(1)}, u32[]{:S(2)}, u32[]{:S(2)}) %collective-permute-start.11) | collective-permute-done | bytes 225312 | tf_op jit(solution)/shard_map/ppermute | solution.py:69
  242.6 1.3 fusion.25
  243.9 1.9 collective-permute-start.14
  245.8 5.3 %collective-permute-start.15 = (bf16[1,704,512]{2,1,0:T(8,128)(2,1)}, bf16[1,704,512]{2,1,0:T(8,128)(2,1)}, u32[]{:S(2)}, u32[]{:S(2)}) collective-permute-start(bf16[1,704,512]{2,1,0:T(8,128)(2,1)} %param.21), channel_id=1, source_target_pairs={{0,8},{8,0},{16,24},{24,16},{32,40},{40,32},{48,56},{56,48},{64,72... | collective-permute-start | bytes 2162696 | tf_op jit(solution)/shard_map/ppermute | solution.py:96
  252.7 15.5 %collective-permute-done.15 = bf16[1,704,512]{2,1,0:T(8,128)(2,1)} collective-permute-done((bf16[1,704,512]{2,1,0:T(8,128)(2,1)}, bf16[1,704,512]{2,1,0:T(8,128)(2,1)}, u32[]{:S(2)}, u32[]{:S(2)}) %collective-permute-start.15) | collective-permute-done | bytes 720928 | tf_op jit(solution)/shard_map/ppermute | solution.py:96
  268.2 2.3 copy.169
  270.5 3.1 fusion.14
  273.6 1.2 reshape.540
  274.8 7.9 %all-to-all-start.1 = ((bf16[1,64,10,512]{3,2,0,1:T(8,128)(2,1)}), bf16[1,64,10,512]{3,2,0,1:T(8,128)(2,1)S(1)}, u32[]{:S(2)}, u32[]{:S(2)}) async-start(bf16[1,64,10,512]{3,2,0,1:T(8,128)(2,1)} %bitcast.30), calls=%async_computation.1 | async-start | bytes 2097152 | tf_op jit(solution)/shard_map/all_to_all | solution.py:180
  283.2 53.2 %all-to-all-done.1 = bf16[1,64,10,512]{3,2,0,1:T(8,128)(2,1)S(1)} async-done(((bf16[1,64,10,512]{3,2,0,1:T(8,128)(2,1)}), bf16[1,64,10,512]{3,2,0,1:T(8,128)(2,1)S(1)}, u32[]{:S(2)}, u32[]{:S(2)}) %all-to-all-start.1) | async-done | bytes 655392 | tf_op jit(solution)/shard_map/all_to_all | solution.py:180
  336.5 1.6 gather_fusion
  338.8 1.3 multiply_reduce_fusion
  (122 shorter events, 19.9 us)
Async XLA Ops:
  0.0 73.1 %copy-start = (bf16[256,512]{1,0:T(8,128)(2,1)S(1)}, bf16[256,512]{1,0:T(8,128)(2,1)}, u32[]{:S(2)}) copy-start(bf16[256,512]{1,0:T(8,128)(2,1)} %param.12) | copy-start | bytes 786436
  5.1 15.3 %collective-permute-start = (bf16[4,130,128]{2,1,0:T(8,128)(2,1)S(1)}, bf16[4,130,128]{2,1,0:T(8,128)(2,1)S(1)}, u32[]{:S(2)}, u32[]{:S(2)}) collective-permute-start(bf16[4,130,128]{2,1,0:T(8,128)(2,1)S(1)} %pad_maximum_fusion.1), channel_id=1, source_target_pairs={{0,8},{8,16},{16,24},{24,32},{32,40},{40,48},{48,56},{56,64},{64,7... | collective-permute-start | bytes 399368 | tf_op jit(solution)/shard_map/ppermute | solution.py:31
  20.8 52.3 %copy-start.3 = (bf16[256,512]{1,0:T(8,128)(2,1)S(1)}, bf16[256,512]{1,0:T(8,128)(2,1)}, u32[]{:S(2)}) copy-start(bf16[256,512]{1,0:T(8,128)(2,1)} %param.14) | copy-start | bytes 786436
  20.9 12.2 %collective-permute-start.1 = (bf16[4,130,128]{2,1,0:T(8,128)(2,1)S(1)}, bf16[4,130,128]{2,1,0:T(8,128)(2,1)S(1)}, u32[]{:S(2)}, u32[]{:S(2)}) collective-permute-start(bf16[4,130,128]{2,1,0:T(8,128)(2,1)S(1)} %pad_maximum_fusion.2), channel_id=1, source_target_pairs={{0,16},{8,24},{16,32},{24,40},{32,48},{40,56},{48,64},{56,72},{64,... | collective-permute-start | bytes 399368 | tf_op jit(solution)/shard_map/ppermute | solution.py:31
  33.7 17.3 %collective-permute-start.2 = (bf16[4,130,128]{2,1,0:T(8,128)(2,1)S(1)}, bf16[4,130,128]{2,1,0:T(8,128)(2,1)S(1)}, u32[]{:S(2)}, u32[]{:S(2)}) collective-permute-start(bf16[4,130,128]{2,1,0:T(8,128)(2,1)S(1)} %pad_maximum_fusion.3), channel_id=1, source_target_pairs={{0,32},{8,40},{16,48},{24,56},{32,64},{40,72},{48,80},{56,88},{64,... | collective-permute-start | bytes 399368 | tf_op jit(solution)/shard_map/ppermute | solution.py:31
  51.5 19.8 %collective-permute-start.3 = (bf16[4,130,128]{2,1,0:T(8,128)(2,1)S(1)}, bf16[4,130,128]{2,1,0:T(8,128)(2,1)S(1)}, u32[]{:S(2)}, u32[]{:S(2)}) collective-permute-start(bf16[4,130,128]{2,1,0:T(8,128)(2,1)S(1)} %pad_maximum_fusion.4), channel_id=1, source_target_pairs={{0,64},{8,72},{16,80},{24,88},{32,96},{40,104},{48,112},{56,120},{... | collective-permute-start | bytes 399368 | tf_op jit(solution)/shard_map/ppermute | solution.py:31
  53.4 43.2 %collective-permute-start.6 = (bf16[1,512,1408]{2,1,0:T(8,128)(2,1)}, bf16[1,512,1408]{2,1,0:T(8,128)(2,1)}, u32[]{:S(2)}, u32[]{:S(2)}) collective-permute-start(bf16[1,512,1408]{2,1,0:T(8,128)(2,1)} %param.20), channel_id=1, source_target_pairs={{0,8},{8,0},{16,24},{24,16},{32,40},{40,32},{48,56},{56,48},{64,72... | collective-permute-start | bytes 4325384 | tf_op jit(solution)/shard_map/ppermute | solution.py:95
  71.7 2.0 copy-start.5
  71.8 7.2 %collective-permute-start.4 = (bf16[4,130,128]{2,1,0:T(8,128)(2,1)S(1)}, bf16[4,130,128]{2,1,0:T(8,128)(2,1)S(1)}, u32[]{:S(2)}, u32[]{:S(2)}) collective-permute-start(bf16[4,130,128]{2,1,0:T(8,128)(2,1)S(1)} %pad_maximum_fusion.5), channel_id=1, source_target_pairs={{0,128},{8,136},{16,144},{24,152},{32,160},{40,168},{48,176},{56,1... | collective-permute-start | bytes 399368 | tf_op jit(solution)/shard_map/ppermute | solution.py:31
  79.5 8.5 %collective-permute-start.5 = (bf16[4,130,128]{2,1,0:T(8,128)(2,1)S(1)}, bf16[4,130,128]{2,1,0:T(8,128)(2,1)S(1)}, u32[]{:S(2)}, u32[]{:S(2)}) collective-permute-start(bf16[4,130,128]{2,1,0:T(8,128)(2,1)S(1)} %pad_maximum_fusion.6), channel_id=1, source_target_pairs={{0,256},{8,264},{16,272},{24,280},{32,288},{40,296},{48,304},{56,3... | collective-permute-start | bytes 399368 | tf_op jit(solution)/shard_map/ppermute | solution.py:31
  96.5 1.0 copy-start.4
  96.6 1.0 copy-start.6
  97.0 13.1 %copy-start.8 = (f32[512]{0:T(512)S(1)}, f32[512]{0:T(512)}, u32[]{:S(2)}) copy-start(f32[512]{0:T(512)} %param.17) | copy-start | bytes 6148
  111.7 64.1 %all-to-all-start = ((bf16[64,1,10,512]{3,2,1,0:T(8,128)(2,1)}), bf16[64,1,10,512]{3,2,1,0:T(8,128)(2,1)S(1)}, u32[]{:S(2)}, u32[]{:S(2)}) async-start(bf16[64,1,10,512]{3,2,1,0:T(8,128)(2,1)} %bitcast.8), calls=%async_computation | async-start | bytes 2097152 | tf_op jit(solution)/shard_map/all_to_all | solution.py:162
  181.2 1.8 copy-start.2
  183.0 6.0 %collective-permute-start.7 = (bf16[1,4,80,2816]{3,2,1,0:T(8,128)(2,1)}, bf16[1,4,80,2816]{3,2,1,0:T(8,128)(2,1)}, u32[]{:S(2)}, u32[]{:S(2)}) collective-permute-start(bf16[1,4,80,2816]{3,2,1,0:T(8,128)(2,1)} %fusion.3), channel_id=1, source_target_pairs={{0,1},{1,0},{2,3},{3,2},{4,5},{5,4},{6,7},{7,6},{8,9},{9,8},{10,11... | collective-permute-start | bytes 5406728 | tf_op jit(solution)/shard_map/ppermute | solution.py:56
  191.0 1.8 copy-start.1
  192.9 15.1 %collective-permute-start.10 = (bf16[1,80,2816]{2,1,0:T(8,128)(2,1)S(1)}, bf16[1,80,2816]{2,1,0:T(8,128)(2,1)S(1)}, u32[]{:S(2)}, u32[]{:S(2)}) collective-permute-start(bf16[1,80,2816]{2,1,0:T(8,128)(2,1)S(1)} %get-tuple-element.44), channel_id=1, source_target_pairs={{0,6},{1,7},{2,0},{3,1},{4,2},{5,3},{6,4},{7,5},{8,14},{9,15},{10,... | collective-permute-start | bytes 1351688 | tf_op jit(solution)/shard_map/ppermute | solution.py:62
  194.8 16.6 %collective-permute-start.9 = (bf16[1,80,2816]{2,1,0:T(8,128)(2,1)S(1)}, bf16[1,80,2816]{2,1,0:T(8,128)(2,1)S(1)}, u32[]{:S(2)}, u32[]{:S(2)}) collective-permute-start(bf16[1,80,2816]{2,1,0:T(8,128)(2,1)S(1)} %get-tuple-element.45), channel_id=1, source_target_pairs={{0,4},{1,5},{2,6},{3,7},{4,0},{5,1},{6,2},{7,3},{8,12},{9,13},{10,... | collective-permute-start | bytes 1351688 | tf_op jit(solution)/shard_map/ppermute | solution.py:62
  198.5 21.8 %collective-permute-start.8 = (bf16[1,80,2816]{2,1,0:T(8,128)(2,1)S(1)}, bf16[1,80,2816]{2,1,0:T(8,128)(2,1)S(1)}, u32[]{:S(2)}, u32[]{:S(2)}) collective-permute-start(bf16[1,80,2816]{2,1,0:T(8,128)(2,1)S(1)} %get-tuple-element.43), channel_id=1, source_target_pairs={{0,2},{1,3},{2,4},{3,5},{4,6},{5,7},{6,0},{7,1},{8,10},{9,11},{10,... | collective-permute-start | bytes 1351688 | tf_op jit(solution)/shard_map/ppermute | solution.py:62
  224.8 10.3 %collective-permute-start.13 = (bf16[1,80,1408]{2,1,0:T(8,128)(2,1)S(1)}, bf16[1,80,1408]{2,1,0:T(8,128)(2,1)S(1)}, u32[]{:S(2)}, u32[]{:S(2)}) collective-permute-start(bf16[1,80,1408]{2,1,0:T(8,128)(2,1)S(1)} %multiply_convert_fusion.1), channel_id=1, source_target_pairs={{0,6},{1,7},{2,0},{3,1},{4,2},{5,3},{6,4},{7,5},{8,14},{9,15},{10,... | collective-permute-start | bytes 675848 | tf_op jit(solution)/shard_map/ppermute | solution.py:69
  227.3 11.0 %collective-permute-start.12 = (bf16[1,80,1408]{2,1,0:T(8,128)(2,1)S(1)}, bf16[1,80,1408]{2,1,0:T(8,128)(2,1)S(1)}, u32[]{:S(2)}, u32[]{:S(2)}) collective-permute-start(bf16[1,80,1408]{2,1,0:T(8,128)(2,1)S(1)} %multiply_convert_fusion.1), channel_id=1, source_target_pairs={{0,4},{1,5},{2,6},{3,7},{4,0},{5,1},{6,2},{7,3},{8,12},{9,13},{10,... | collective-permute-start | bytes 675848 | tf_op jit(solution)/shard_map/ppermute | solution.py:69
  230.9 11.5 %collective-permute-start.11 = (bf16[1,80,1408]{2,1,0:T(8,128)(2,1)S(1)}, bf16[1,80,1408]{2,1,0:T(8,128)(2,1)S(1)}, u32[]{:S(2)}, u32[]{:S(2)}) collective-permute-start(bf16[1,80,1408]{2,1,0:T(8,128)(2,1)S(1)} %multiply_convert_fusion.1), channel_id=1, source_target_pairs={{0,2},{1,3},{2,4},{3,5},{4,6},{5,7},{6,0},{7,1},{8,10},{9,11},{10,... | collective-permute-start | bytes 675848 | tf_op jit(solution)/shard_map/ppermute | solution.py:69
  243.9 7.6 %collective-permute-start.14 = (bf16[1,4,80,1408]{3,2,1,0:T(8,128)(2,1)}, bf16[1,4,80,1408]{3,2,1,0:T(8,128)(2,1)S(1)}, u32[]{:S(2)}, u32[]{:S(2)}) collective-permute-start(bf16[1,4,80,1408]{3,2,1,0:T(8,128)(2,1)} %fusion.25), channel_id=1, source_target_pairs={{0,1},{1,0},{2,3},{3,2},{4,5},{5,4},{6,7},{7,6},{8,9},{9,8},{10,11... | collective-permute-start | bytes 2703368 | tf_op jit(solution)/shard_map/ppermute | solution.py:74
  245.8 22.4 %collective-permute-start.15 = (bf16[1,704,512]{2,1,0:T(8,128)(2,1)}, bf16[1,704,512]{2,1,0:T(8,128)(2,1)}, u32[]{:S(2)}, u32[]{:S(2)}) collective-permute-start(bf16[1,704,512]{2,1,0:T(8,128)(2,1)} %param.21), channel_id=1, source_target_pairs={{0,8},{8,0},{16,24},{24,16},{32,40},{40,32},{48,56},{56,48},{64,72... | collective-permute-start | bytes 2162696 | tf_op jit(solution)/shard_map/ppermute | solution.py:96
  273.6 9.4 %copy-start.7 = (f32[256,2]{0,1:T(2,128)S(1)}, f32[256,2]{0,1:T(2,128)}, u32[]{:S(2)}) copy-start(f32[256,2]{0,1:T(2,128)} %param.19) | copy-start | bytes 6148
  274.8 61.5 %all-to-all-start.1 = ((bf16[1,64,10,512]{3,2,0,1:T(8,128)(2,1)}), bf16[1,64,10,512]{3,2,0,1:T(8,128)(2,1)S(1)}, u32[]{:S(2)}, u32[]{:S(2)}) async-start(bf16[1,64,10,512]{3,2,0,1:T(8,128)(2,1)} %bitcast.30), calls=%async_computation.1 | async-start | bytes 2097152 | tf_op jit(solution)/shard_map/all_to_all | solution.py:180
where the time goes:
time: 342 us; the launch traced here: 341 us
  waiting for transfers between devices  217 us (63%)
  starting transfers between devices  67.1 us (20%)
  local copies, waits for them, and re-layouts  18.2 us (5%)
  other arithmetic  13.8 us (4%)
  blocking collectives  12.4 us (4%)
  matrix products  11.1 us (3%)
    ppermute x6, waiting for transfers between devices, exclusive_scan(): got = lax.ppermute(pack_window(window_decay, window_state), axis, pairs)  59.5 us
    all_to_all x1, waiting for transfers between devices, per_device(): lax.all_to_all(summed, 'seq', split_axis=1, concat_axis=0, tiled=True)  53.2 us
    all_to_all x1, waiting for transfers between devices, per_device(): lax.all_to_all(send_buffer, 'seq', split_axis=0, concat_axis=1, tiled=True)  50.7 us
    ppermute x3, waiting for transfers between devices, head_reduce_activate(): total = total + lax.ppermute(outgoing, axis, pairs).astype(jnp.float32)  18.4 us
    ppermute x1, waiting for transfers between devices, per_device(): other_out = lax.ppermute(expert_out, 'seq', partner)  15.5 us
    all_to_all x1, starting transfers between devices, per_device(): lax.all_to_all(send_buffer, 'seq', split_axis=0, concat_axis=1, tiled=True)  13.4 us
    psum x1, blocking collectives, per_device(): total_squares = lax.psum(local_squares, 'head')  12.4 us
    ppermute x6, starting transfers between devices, exclusive_scan(): got = lax.ppermute(pack_window(window_decay, window_state), axis, pairs)  12.2 us
  transfers between devices with their start and end apart: 18, of which 17 were waited for; matrix products, arithmetic and copies ran while one was open for 2% of the time, Pallas kernels for 0%

commit v1 on v0

--- a/solution.py
+++ b/solution.py
@@ -134,7 +134,7 @@
     hidden_state = (tokens.astype(jnp.float32) + normed_heads * head_gain).astype(jnp.bfloat16)
     hidden_wide = hidden_state.astype(jnp.float32)
     local_squares = jnp.sum(hidden_wide * hidden_wide, axis=1)
-    total_squares = lax.psum(local_squares, "head")
+    total_squares = jnp.sum(lax.all_gather(local_squares, "head"), axis=0)
     inverse_rms = lax.rsqrt(total_squares / D + EPSILON)
     expert_input = (hidden_wide * inverse_rms[:, None] * expert_gain).astype(jnp.bfloat16)
     capacity = CAP

time: 342 us -> 339 us (level)
  waiting for transfers between devices: 217 us -> 223 us
  starting transfers between devices: 67.1 us -> 61.2 us
    psum x1 -> x0, blocking collectives: 12.4 us -> none  [per_device(): total_squares = lax.psum(local_squares, 'head')]
    all_gather x0 -> x1, blocking collectives: none -> 9.78 us  [per_device(): total_squares = jnp.sum(lax.all_gather(local_squares, 'head'), axis=0)]
    all_to_all x1, waiting for transfers between devices: 50.7 us -> 54.4 us  [per_device(): lax.all_to_all(send_buffer, 'seq', split_axis=0, concat_axis=1, tiled=True)]
where the time goes in v1:
time: 339 us; the launch traced here: 338 us
  waiting for transfers between devices  223 us (66%)
  starting transfers between devices  61.2 us (18%)
  local copies, waits for them, and re-layouts  18.2 us (5%)
  other arithmetic  13.9 us (4%)
  matrix products  11.1 us (3%)
  blocking collectives  9.78 us (3%)
    ppermute x6, waiting for transfers between devices, exclusive_scan(): got = lax.ppermute(pack_window(window_decay, window_state), axis, pairs)  59.5 us
    all_to_all x1, waiting for transfers between devices, per_device(): lax.all_to_all(send_buffer, 'seq', split_axis=0, concat_axis=1, tiled=True)  54.4 us
    all_to_all x1, waiting for transfers between devices, per_device(): lax.all_to_all(summed, 'seq', split_axis=1, concat_axis=0, tiled=True)  53.2 us
    ppermute x3, waiting for transfers between devices, head_reduce_activate(): total = total + lax.ppermute(outgoing, axis, pairs).astype(jnp.float32)  19.2 us
    ppermute x1, waiting for transfers between devices, per_device(): other_out = lax.ppermute(expert_out, 'seq', partner)  16.1 us
    all_to_all x1, starting transfers between devices, per_device(): lax.all_to_all(send_buffer, 'seq', split_axis=0, concat_axis=1, tiled=True)  12.2 us
    ppermute x6, starting transfers between devices, exclusive_scan(): got = lax.ppermute(pack_window(window_decay, window_state), axis, pairs)  12.2 us
    all_gather x1, blocking collectives, per_device(): total_squares = jnp.sum(lax.all_gather(local_squares, 'head'), axis=0)  9.78 us
  transfers between devices with their start and end apart: 18, of which 17 were waited for; matrix products, arithmetic and copies ran while one was open for 2% of the time, Pallas kernels for 0%

profile of v1, /device:TPU:6, one launch (start us, length us, event | category | flops | bytes accessed | tf_op | source)
XLA Modules:
  0.0 338.0 jit_solution(936194519044418843)
XLA Ops:
  1.8 1.2 reduce-window.6
  5.1 3.8 %collective-permute-start = (bf16[4,130,128]{2,1,0:T(8,128)(2,1)S(1)}, bf16[4,130,128]{2,1,0:T(8,128)(2,1)S(1)}, u32[]{:S(2)}, u32[]{:S(2)}) collective-permute-start(bf16[4,130,128]{2,1,0:T(8,128)(2,1)S(1)} %pad_maximum_fusion.1), channel_id=1, source_target_pairs={{0,8},{8,16},{16,24},{24,32},{32,40},{40,48},{48,56},{56,64},{64,7... | collective-permute-start | bytes 399368 | tf_op jit(solution)/shard_map/ppermute | solution.py:31
  9.0 11.5 %collective-permute-done = bf16[4,130,128]{2,1,0:T(8,128)(2,1)S(1)} collective-permute-done((bf16[4,130,128]{2,1,0:T(8,128)(2,1)S(1)}, bf16[4,130,128]{2,1,0:T(8,128)(2,1)S(1)}, u32[]{:S(2)}, u32[]{:S(2)}) %collective-permute-start) | collective-permute-done | bytes 133152 | tf_op jit(solution)/shard_map/ppermute | solution.py:31
  20.9 1.9 collective-permute-start.1
  22.9 10.1 %collective-permute-done.1 = bf16[4,130,128]{2,1,0:T(8,128)(2,1)S(1)} collective-permute-done((bf16[4,130,128]{2,1,0:T(8,128)(2,1)S(1)}, bf16[4,130,128]{2,1,0:T(8,128)(2,1)S(1)}, u32[]{:S(2)}, u32[]{:S(2)}) %collective-permute-start.1) | collective-permute-done | bytes 133152 | tf_op jit(solution)/shard_map/ppermute | solution.py:31
  33.7 1.9 collective-permute-start.2
  35.6 15.3 %collective-permute-done.2 = bf16[4,130,128]{2,1,0:T(8,128)(2,1)S(1)} collective-permute-done((bf16[4,130,128]{2,1,0:T(8,128)(2,1)S(1)}, bf16[4,130,128]{2,1,0:T(8,128)(2,1)S(1)}, u32[]{:S(2)}, u32[]{:S(2)}) %collective-permute-start.2) | collective-permute-done | bytes 133152 | tf_op jit(solution)/shard_map/ppermute | solution.py:31
  51.5 1.9 collective-permute-start.3
  53.4 6.7 %collective-permute-start.6 = (bf16[1,512,1408]{2,1,0:T(8,128)(2,1)}, bf16[1,512,1408]{2,1,0:T(8,128)(2,1)}, u32[]{:S(2)}, u32[]{:S(2)}) collective-permute-start(bf16[1,512,1408]{2,1,0:T(8,128)(2,1)} %param.20), channel_id=1, source_target_pairs={{0,8},{8,0},{16,24},{24,16},{32,40},{40,32},{48,56},{56,48},{64,72... | collective-permute-start | bytes 4325384 | tf_op jit(solution)/shard_map/ppermute | solution.py:95
  60.2 11.1 %collective-permute-done.3 = bf16[4,130,128]{2,1,0:T(8,128)(2,1)S(1)} collective-permute-done((bf16[4,130,128]{2,1,0:T(8,128)(2,1)S(1)}, bf16[4,130,128]{2,1,0:T(8,128)(2,1)S(1)}, u32[]{:S(2)}, u32[]{:S(2)}) %collective-permute-start.3) | collective-permute-done | bytes 133152 | tf_op jit(solution)/shard_map/ppermute | solution.py:31
  71.8 1.3 collective-permute-start.4
  74.5 4.5 %collective-permute-done.4 = bf16[4,130,128]{2,1,0:T(8,128)(2,1)S(1)} collective-permute-done((bf16[4,130,128]{2,1,0:T(8,128)(2,1)S(1)}, bf16[4,130,128]{2,1,0:T(8,128)(2,1)S(1)}, u32[]{:S(2)}, u32[]{:S(2)}) %collective-permute-start.4) | collective-permute-done | bytes 133152 | tf_op jit(solution)/shard_map/ppermute | solution.py:31
  79.5 1.3 collective-permute-start.5
  81.0 6.9 %collective-permute-done.5 = bf16[4,130,128]{2,1,0:T(8,128)(2,1)S(1)} collective-permute-done((bf16[4,130,128]{2,1,0:T(8,128)(2,1)S(1)}, bf16[4,130,128]{2,1,0:T(8,128)(2,1)S(1)}, u32[]{:S(2)}, u32[]{:S(2)}) %collective-permute-start.5) | collective-permute-done | bytes 133152 | tf_op jit(solution)/shard_map/ppermute | solution.py:31
  88.2 8.4 %collective-permute-done.6 = bf16[1,512,1408]{2,1,0:T(8,128)(2,1)} collective-permute-done((bf16[1,512,1408]{2,1,0:T(8,128)(2,1)}, bf16[1,512,1408]{2,1,0:T(8,128)(2,1)}, u32[]{:S(2)}, u32[]{:S(2)}) %collective-permute-start.6) | collective-permute-done | bytes 1441824 | tf_op jit(solution)/shard_map/ppermute | solution.py:95
  97.7 9.8 %all-gather.1 = f32[8,1,256]{2,1,0:T(1,128)S(1)} all-gather(f32[1,1,256]{2,1,0:T(1,128)S(1)} %bitcast.167), channel_id=2, replica_groups=mesh['seq'=64,'head'=8] {'head'}, dimensions={0}, use_global_device_ids=true | all-gather | bytes 9216 | tf_op jit(solution)/shard_map/all_gather | solution.py:137
  109.1 12.2 %all-to-all-start = ((bf16[64,1,10,512]{3,2,1,0:T(8,128)(2,1)}), bf16[64,1,10,512]{3,2,1,0:T(8,128)(2,1)S(1)}, u32[]{:S(2)}, u32[]{:S(2)}) async-start(bf16[64,1,10,512]{3,2,1,0:T(8,128)(2,1)} %bitcast.9), calls=%async_computation | async-start | bytes 2097152 | tf_op jit(solution)/shard_map/all_to_all | solution.py:162
  121.3 54.4 %all-to-all-done = bf16[64,1,10,512]{3,2,1,0:T(8,128)(2,1)S(1)} async-done(((bf16[64,1,10,512]{3,2,1,0:T(8,128)(2,1)}), bf16[64,1,10,512]{3,2,1,0:T(8,128)(2,1)S(1)}, u32[]{:S(2)}, u32[]{:S(2)}) %all-to-all-start) | async-done | bytes 655392 | tf_op jit(solution)/shard_map/all_to_all | solution.py:162
  176.0 2.5 convolution_convert_fusion.1
  178.5 2.5 convolution_convert_fusion
  181.1 1.5 fusion.3
  182.9 1.9 collective-permute-start.7
  184.9 4.0 %collective-permute-done.7 = bf16[1,4,80,2816]{3,2,1,0:T(8,128)(2,1)} collective-permute-done((bf16[1,4,80,2816]{3,2,1,0:T(8,128)(2,1)}, bf16[1,4,80,2816]{3,2,1,0:T(8,128)(2,1)}, u32[]{:S(2)}, u32[]{:S(2)}) %collective-permute-start.7) | collective-permute-done | bytes 1802272 | tf_op jit(solution)/shard_map/ppermute | solution.py:56
  188.9 2.1 convert_add_fusion
  191.0 1.8 copy-done.1
  192.9 1.9 collective-permute-start.10
  194.8 3.4 %collective-permute-start.9 = (bf16[1,80,2816]{2,1,0:T(8,128)(2,1)S(1)}, bf16[1,80,2816]{2,1,0:T(8,128)(2,1)S(1)}, u32[]{:S(2)}, u32[]{:S(2)}) collective-permute-start(bf16[1,80,2816]{2,1,0:T(8,128)(2,1)S(1)} %get-tuple-element.45), channel_id=1, source_target_pairs={{0,4},{1,5},{2,6},{3,7},{4,0},{5,1},{6,2},{7,3},{8,12},{9,13},{10,... | collective-permute-start | bytes 1351688 | tf_op jit(solution)/shard_map/ppermute | solution.py:62
  198.2 2.8 collective-permute-start.8
  201.0 6.9 %collective-permute-done.10 = bf16[1,80,2816]{2,1,0:T(8,128)(2,1)S(1)} collective-permute-done((bf16[1,80,2816]{2,1,0:T(8,128)(2,1)S(1)}, bf16[1,80,2816]{2,1,0:T(8,128)(2,1)S(1)}, u32[]{:S(2)}, u32[]{:S(2)}) %collective-permute-start.10) | collective-permute-done | bytes 450592 | tf_op jit(solution)/shard_map/ppermute | solution.py:62
  207.9 3.5 %collective-permute-done.9 = bf16[1,80,2816]{2,1,0:T(8,128)(2,1)S(1)} collective-permute-done((bf16[1,80,2816]{2,1,0:T(8,128)(2,1)S(1)}, bf16[1,80,2816]{2,1,0:T(8,128)(2,1)S(1)}, u32[]{:S(2)}, u32[]{:S(2)}) %collective-permute-start.9) | collective-permute-done | bytes 450592 | tf_op jit(solution)/shard_map/ppermute | solution.py:62
  211.4 8.8 %collective-permute-done.8 = bf16[1,80,2816]{2,1,0:T(8,128)(2,1)S(1)} collective-permute-done((bf16[1,80,2816]{2,1,0:T(8,128)(2,1)S(1)}, bf16[1,80,2816]{2,1,0:T(8,128)(2,1)S(1)}, u32[]{:S(2)}, u32[]{:S(2)}) %collective-permute-start.8) | collective-permute-done | bytes 450592 | tf_op jit(solution)/shard_map/ppermute | solution.py:62
  220.2 1.4 fusion.27
  224.7 2.5 collective-permute-start.13
  227.2 3.2 collective-permute-start.12
  230.4 2.7 collective-permute-start.11
  235.0 3.3 collective-permute-done.12
  238.3 4.0 %collective-permute-done.11 = bf16[1,80,1408]{2,1,0:T(8,128)(2,1)S(1)} collective-permute-done((bf16[1,80,1408]{2,1,0:T(8,128)(2,1)S(1)}, bf16[1,80,1408]{2,1,0:T(8,128)(2,1)S(1)}, u32[]{:S(2)}, u32[]{:S(2)}) %collective-permute-start.11) | collective-permute-done | bytes 225312 | tf_op jit(solution)/shard_map/ppermute | solution.py:69
  242.5 1.3 fusion.25
  243.8 1.9 collective-permute-start.14
  245.8 3.1 collective-permute-start.15
  250.4 16.1 %collective-permute-done.15 = bf16[1,704,512]{2,1,0:T(8,128)(2,1)} collective-permute-done((bf16[1,704,512]{2,1,0:T(8,128)(2,1)}, bf16[1,704,512]{2,1,0:T(8,128)(2,1)}, u32[]{:S(2)}, u32[]{:S(2)}) %collective-permute-start.15) | collective-permute-done | bytes 720928 | tf_op jit(solution)/shard_map/ppermute | solution.py:96
  266.5 2.3 copy.169
  268.8 3.1 fusion.14
  271.9 1.2 reshape.544
  273.1 6.7 %all-to-all-start.1 = ((bf16[1,64,10,512]{3,2,0,1:T(8,128)(2,1)}), bf16[1,64,10,512]{3,2,0,1:T(8,128)(2,1)S(1)}, u32[]{:S(2)}, u32[]{:S(2)}) async-start(bf16[1,64,10,512]{3,2,0,1:T(8,128)(2,1)} %bitcast.31), calls=%async_computation.1 | async-start | bytes 2097152 | tf_op jit(solution)/shard_map/all_to_all | solution.py:180
  280.2 53.2 %all-to-all-done.1 = bf16[1,64,10,512]{3,2,0,1:T(8,128)(2,1)S(1)} async-done(((bf16[1,64,10,512]{3,2,0,1:T(8,128)(2,1)}), bf16[1,64,10,512]{3,2,0,1:T(8,128)(2,1)S(1)}, u32[]{:S(2)}, u32[]{:S(2)}) %all-to-all-start.1) | async-done | bytes 655392 | tf_op jit(solution)/shard_map/all_to_all | solution.py:180
  333.6 1.6 gather_fusion
  335.9 1.3 multiply_reduce_fusion
  (123 shorter events, 20.3 us)
Async XLA Ops:
  0.0 73.1 %copy-start = (bf16[256,512]{1,0:T(8,128)(2,1)S(1)}, bf16[256,512]{1,0:T(8,128)(2,1)}, u32[]{:S(2)}) copy-start(bf16[256,512]{1,0:T(8,128)(2,1)} %param.12) | copy-start | bytes 786436
  5.1 15.3 %collective-permute-start = (bf16[4,130,128]{2,1,0:T(8,128)(2,1)S(1)}, bf16[4,130,128]{2,1,0:T(8,128)(2,1)S(1)}, u32[]{:S(2)}, u32[]{:S(2)}) collective-permute-start(bf16[4,130,128]{2,1,0:T(8,128)(2,1)S(1)} %pad_maximum_fusion.1), channel_id=1, source_target_pairs={{0,8},{8,16},{16,24},{24,32},{32,40},{40,48},{48,56},{56,64},{64,7... | collective-permute-start | bytes 399368 | tf_op jit(solution)/shard_map/ppermute | solution.py:31
  20.8 52.3 %copy-start.3 = (bf16[256,512]{1,0:T(8,128)(2,1)S(1)}, bf16[256,512]{1,0:T(8,128)(2,1)}, u32[]{:S(2)}) copy-start(bf16[256,512]{1,0:T(8,128)(2,1)} %param.14) | copy-start | bytes 786436
  20.9 12.2 %collective-permute-start.1 = (bf16[4,130,128]{2,1,0:T(8,128)(2,1)S(1)}, bf16[4,130,128]{2,1,0:T(8,128)(2,1)S(1)}, u32[]{:S(2)}, u32[]{:S(2)}) collective-permute-start(bf16[4,130,128]{2,1,0:T(8,128)(2,1)S(1)} %pad_maximum_fusion.2), channel_id=1, source_target_pairs={{0,16},{8,24},{16,32},{24,40},{32,48},{40,56},{48,64},{56,72},{64,... | collective-permute-start | bytes 399368 | tf_op jit(solution)/shard_map/ppermute | solution.py:31
  33.7 17.3 %collective-permute-start.2 = (bf16[4,130,128]{2,1,0:T(8,128)(2,1)S(1)}, bf16[4,130,128]{2,1,0:T(8,128)(2,1)S(1)}, u32[]{:S(2)}, u32[]{:S(2)}) collective-permute-start(bf16[4,130,128]{2,1,0:T(8,128)(2,1)S(1)} %pad_maximum_fusion.3), channel_id=1, source_target_pairs={{0,32},{8,40},{16,48},{24,56},{32,64},{40,72},{48,80},{56,88},{64,... | collective-permute-start | bytes 399368 | tf_op jit(solution)/shard_map/ppermute | solution.py:31
  51.5 19.8 %collective-permute-start.3 = (bf16[4,130,128]{2,1,0:T(8,128)(2,1)S(1)}, bf16[4,130,128]{2,1,0:T(8,128)(2,1)S(1)}, u32[]{:S(2)}, u32[]{:S(2)}) collective-permute-start(bf16[4,130,128]{2,1,0:T(8,128)(2,1)S(1)} %pad_maximum_fusion.4), channel_id=1, source_target_pairs={{0,64},{8,72},{16,80},{24,88},{32,96},{40,104},{48,112},{56,120},{... | collective-permute-start | bytes 399368 | tf_op jit(solution)/shard_map/ppermute | solution.py:31
  53.4 43.2 %collective-permute-start.6 = (bf16[1,512,1408]{2,1,0:T(8,128)(2,1)}, bf16[1,512,1408]{2,1,0:T(8,128)(2,1)}, u32[]{:S(2)}, u32[]{:S(2)}) collective-permute-start(bf16[1,512,1408]{2,1,0:T(8,128)(2,1)} %param.20), channel_id=1, source_target_pairs={{0,8},{8,0},{16,24},{24,16},{32,40},{40,32},{48,56},{56,48},{64,72... | collective-permute-start | bytes 4325384 | tf_op jit(solution)/shard_map/ppermute | solution.py:95
  71.7 2.0 copy-start.5
  71.8 7.2 %collective-permute-start.4 = (bf16[4,130,128]{2,1,0:T(8,128)(2,1)S(1)}, bf16[4,130,128]{2,1,0:T(8,128)(2,1)S(1)}, u32[]{:S(2)}, u32[]{:S(2)}) collective-permute-start(bf16[4,130,128]{2,1,0:T(8,128)(2,1)S(1)} %pad_maximum_fusion.5), channel_id=1, source_target_pairs={{0,128},{8,136},{16,144},{24,152},{32,160},{40,168},{48,176},{56,1... | collective-permute-start | bytes 399368 | tf_op jit(solution)/shard_map/ppermute | solution.py:31
  79.5 8.5 %collective-permute-start.5 = (bf16[4,130,128]{2,1,0:T(8,128)(2,1)S(1)}, bf16[4,130,128]{2,1,0:T(8,128)(2,1)S(1)}, u32[]{:S(2)}, u32[]{:S(2)}) collective-permute-start(bf16[4,130,128]{2,1,0:T(8,128)(2,1)S(1)} %pad_maximum_fusion.6), channel_id=1, source_target_pairs={{0,256},{8,264},{16,272},{24,280},{32,288},{40,296},{48,304},{56,3... | collective-permute-start | bytes 399368 | tf_op jit(solution)/shard_map/ppermute | solution.py:31
  96.5 1.0 copy-start.4
  96.6 1.0 copy-start.6
  97.0 10.5 %copy-start.8 = (f32[512]{0:T(512)S(1)}, f32[512]{0:T(512)}, u32[]{:S(2)}) copy-start(f32[512]{0:T(512)} %param.17) | copy-start | bytes 6148
  109.1 66.6 %all-to-all-start = ((bf16[64,1,10,512]{3,2,1,0:T(8,128)(2,1)}), bf16[64,1,10,512]{3,2,1,0:T(8,128)(2,1)S(1)}, u32[]{:S(2)}, u32[]{:S(2)}) async-start(bf16[64,1,10,512]{3,2,1,0:T(8,128)(2,1)} %bitcast.9), calls=%async_computation | async-start | bytes 2097152 | tf_op jit(solution)/shard_map/all_to_all | solution.py:162
  181.1 1.8 copy-start.2
  182.9 6.0 %collective-permute-start.7 = (bf16[1,4,80,2816]{3,2,1,0:T(8,128)(2,1)}, bf16[1,4,80,2816]{3,2,1,0:T(8,128)(2,1)}, u32[]{:S(2)}, u32[]{:S(2)}) collective-permute-start(bf16[1,4,80,2816]{3,2,1,0:T(8,128)(2,1)} %fusion.3), channel_id=1, source_target_pairs={{0,1},{1,0},{2,3},{3,2},{4,5},{5,4},{6,7},{7,6},{8,9},{9,8},{10,11... | collective-permute-start | bytes 5406728 | tf_op jit(solution)/shard_map/ppermute | solution.py:56
  190.9 1.8 copy-start.1
  192.9 15.1 %collective-permute-start.10 = (bf16[1,80,2816]{2,1,0:T(8,128)(2,1)S(1)}, bf16[1,80,2816]{2,1,0:T(8,128)(2,1)S(1)}, u32[]{:S(2)}, u32[]{:S(2)}) collective-permute-start(bf16[1,80,2816]{2,1,0:T(8,128)(2,1)S(1)} %get-tuple-element.44), channel_id=1, source_target_pairs={{0,6},{1,7},{2,0},{3,1},{4,2},{5,3},{6,4},{7,5},{8,14},{9,15},{10,... | collective-permute-start | bytes 1351688 | tf_op jit(solution)/shard_map/ppermute | solution.py:62
  194.8 16.6 %collective-permute-start.9 = (bf16[1,80,2816]{2,1,0:T(8,128)(2,1)S(1)}, bf16[1,80,2816]{2,1,0:T(8,128)(2,1)S(1)}, u32[]{:S(2)}, u32[]{:S(2)}) collective-permute-start(bf16[1,80,2816]{2,1,0:T(8,128)(2,1)S(1)} %get-tuple-element.45), channel_id=1, source_target_pairs={{0,4},{1,5},{2,6},{3,7},{4,0},{5,1},{6,2},{7,3},{8,12},{9,13},{10,... | collective-permute-start | bytes 1351688 | tf_op jit(solution)/shard_map/ppermute | solution.py:62
  198.2 22.0 %collective-permute-start.8 = (bf16[1,80,2816]{2,1,0:T(8,128)(2,1)S(1)}, bf16[1,80,2816]{2,1,0:T(8,128)(2,1)S(1)}, u32[]{:S(2)}, u32[]{:S(2)}) collective-permute-start(bf16[1,80,2816]{2,1,0:T(8,128)(2,1)S(1)} %get-tuple-element.43), channel_id=1, source_target_pairs={{0,2},{1,3},{2,4},{3,5},{4,6},{5,7},{6,0},{7,1},{8,10},{9,11},{10,... | collective-permute-start | bytes 1351688 | tf_op jit(solution)/shard_map/ppermute | solution.py:62
  224.7 10.3 %collective-permute-start.13 = (bf16[1,80,1408]{2,1,0:T(8,128)(2,1)S(1)}, bf16[1,80,1408]{2,1,0:T(8,128)(2,1)S(1)}, u32[]{:S(2)}, u32[]{:S(2)}) collective-permute-start(bf16[1,80,1408]{2,1,0:T(8,128)(2,1)S(1)} %multiply_convert_fusion.1), channel_id=1, source_target_pairs={{0,6},{1,7},{2,0},{3,1},{4,2},{5,3},{6,4},{7,5},{8,14},{9,15},{10,... | collective-permute-start | bytes 675848 | tf_op jit(solution)/shard_map/ppermute | solution.py:69
  227.2 11.0 %collective-permute-start.12 = (bf16[1,80,1408]{2,1,0:T(8,128)(2,1)S(1)}, bf16[1,80,1408]{2,1,0:T(8,128)(2,1)S(1)}, u32[]{:S(2)}, u32[]{:S(2)}) collective-permute-start(bf16[1,80,1408]{2,1,0:T(8,128)(2,1)S(1)} %multiply_convert_fusion.1), channel_id=1, source_target_pairs={{0,4},{1,5},{2,6},{3,7},{4,0},{5,1},{6,2},{7,3},{8,12},{9,13},{10,... | collective-permute-start | bytes 675848 | tf_op jit(solution)/shard_map/ppermute | solution.py:69
  230.4 11.9 %collective-permute-start.11 = (bf16[1,80,1408]{2,1,0:T(8,128)(2,1)S(1)}, bf16[1,80,1408]{2,1,0:T(8,128)(2,1)S(1)}, u32[]{:S(2)}, u32[]{:S(2)}) collective-permute-start(bf16[1,80,1408]{2,1,0:T(8,128)(2,1)S(1)} %multiply_convert_fusion.1), channel_id=1, source_target_pairs={{0,2},{1,3},{2,4},{3,5},{4,6},{5,7},{6,0},{7,1},{8,10},{9,11},{10,... | collective-permute-start | bytes 675848 | tf_op jit(solution)/shard_map/ppermute | solution.py:69
  243.8 5.4 %collective-permute-start.14 = (bf16[1,4,80,1408]{3,2,1,0:T(8,128)(2,1)}, bf16[1,4,80,1408]{3,2,1,0:T(8,128)(2,1)S(1)}, u32[]{:S(2)}, u32[]{:S(2)}) collective-permute-start(bf16[1,4,80,1408]{3,2,1,0:T(8,128)(2,1)} %fusion.25), channel_id=1, source_target_pairs={{0,1},{1,0},{2,3},{3,2},{4,5},{5,4},{6,7},{7,6},{8,9},{9,8},{10,11... | collective-permute-start | bytes 2703368 | tf_op jit(solution)/shard_map/ppermute | solution.py:74
  245.8 20.8 %collective-permute-start.15 = (bf16[1,704,512]{2,1,0:T(8,128)(2,1)}, bf16[1,704,512]{2,1,0:T(8,128)(2,1)}, u32[]{:S(2)}, u32[]{:S(2)}) collective-permute-start(bf16[1,704,512]{2,1,0:T(8,128)(2,1)} %param.21), channel_id=1, source_target_pairs={{0,8},{8,0},{16,24},{24,16},{32,40},{40,32},{48,56},{56,48},{64,72... | collective-permute-start | bytes 2162696 | tf_op jit(solution)/shard_map/ppermute | solution.py:96
  271.9 8.2 %copy-start.7 = (f32[256,2]{0,1:T(2,128)S(1)}, f32[256,2]{0,1:T(2,128)}, u32[]{:S(2)}) copy-start(f32[256,2]{0,1:T(2,128)} %param.19) | copy-start | bytes 6148
  273.1 60.3 %all-to-all-start.1 = ((bf16[1,64,10,512]{3,2,0,1:T(8,128)(2,1)}), bf16[1,64,10,512]{3,2,0,1:T(8,128)(2,1)S(1)}, u32[]{:S(2)}, u32[]{:S(2)}) async-start(bf16[1,64,10,512]{3,2,0,1:T(8,128)(2,1)} %bitcast.31), calls=%async_computation.1 | async-start | bytes 2097152 | tf_op jit(solution)/shard_map/all_to_all | solution.py:180
